TPU v7x, 256 devices: a whole 4x4x8 slice. The times are simulated.
256 devices in a mesh: hyp: 32 (over y, x, core), head: 8 (over z).
Axes of the slice: x: 4, y: 4, z: 8, core: 2. Of those that a mesh axis runs over, the one named last changes fastest.
Arguments:
- step_embeds: bfloat16 [3, 512, 4096], P(None, 'hyp'), may hold values from -6 to 6
- lang_table: bfloat16 [8, 4096], replicated, may hold values from -3 to 3
- lang_ids: int32 [32, 4], replicated, may hold values from 0 to 7
- self_gain: float32 [4096], replicated, may hold values from 0.1 to 1.9
- self_wq: bfloat16 [4096, 2048], P(None, 'head'), may hold values from -0.09375 to 0.09375
- self_wk: bfloat16 [4096, 2048], P(None, 'head'), may hold values from -0.09375 to 0.09375
- self_wv: bfloat16 [4096, 2048], P(None, 'head'), may hold values from -0.09375 to 0.09375
- self_wo: bfloat16 [2048, 4096], P('head'), may hold values from -0.125 to 0.125
- cross_gain: float32 [4096], replicated, may hold values from 0.1 to 1.9
- cross_wq: bfloat16 [4096, 2048], P(None, 'head'), may hold values from -0.09375 to 0.09375
- cross_wkv: bfloat16 [4096, 4096], P('hyp', 'head'), may hold values from -0.09375 to 0.09375
- encoder_rows: bfloat16 [24576, 4096], P('hyp', 'head'), may hold values from -200 to 200
- doc_lengths: int32 [32], P('hyp'), may hold values from 192 to 768, as said below
- past_keys: bfloat16 [512, 32, 2048], P('hyp', None, 'head'), may hold values from -200 to 200
- past_values: bfloat16 [512, 32, 2048], P('hyp', None, 'head'), may hold values from -6 to 6
- parents: int32 [3, 512], replicated, may hold values from 0 to 3
Outputs:
- cross_context: bfloat16 [3, 512, 2048], P(None, 'hyp', 'head')
- final_keys: bfloat16 [512, 35, 2048], P('hyp', None, 'head')
- final_values: bfloat16 [512, 35, 2048], P('hyp', None, 'head')
Inputs may be any that keep to these rules, and one draw needn't show every extreme that they name: `doc_lengths`: some document has exactly 768 live rows. `parents`: A parent is a beam of the same document and target.
All inputs are finite; a program needn't handle non-finite values.
Results may differ from a plain program's by a relative error of at most 0.03.
Values may be sent and summed in bfloat16 or wider, within the bound.
No kernel may reach another device: no remote copies, remote signals or barrier semaphores. Data moves between devices by JAX's collectives and lax.ppermute only.
A program may use at most 128 MiB of HBM per device.

v0:
```python
import jax
import jax.numpy as jnp
from jax import lax
from jax.sharding import PartitionSpec as P

HEAD = 256
BEAMS = 4
TARGETS = 4
STEPS = 3
EPSILON = 1e-06


def shifted(block, axis, distance):
    devices = range(lax.axis_size(axis))
    route = [((i - distance) % len(devices), i) for i in devices]
    return lax.ppermute(block, axis, route)


def rms_scaled(values_in, gain):
    mean_square = jnp.mean(values_in * values_in, axis=-1, keepdims=True)
    return values_in * lax.rsqrt(mean_square + EPSILON) * gain


def pick_rows(candidates, selector, row_axis):
    shape_list = [1] * candidates[0].ndim
    shape_list[row_axis] = selector.shape[0]
    chosen = candidates[0]
    for position in range(1, len(candidates)):
        chosen = jnp.where((selector == position).reshape(shape_list), candidates[position], chosen)
    return chosen


def partial_attend(queries, cache_stack, scaling):
    row_count = cache_stack.shape[1]
    cached = cache_stack.shape[2]
    heads_here = cache_stack.shape[3] // HEAD
    key_part = cache_stack[0].reshape(row_count, cached, heads_here, HEAD)
    value_part = cache_stack[1].reshape(row_count, cached, heads_here, HEAD).astype(jnp.float32)
    scores = (
        jnp.einsum(
            "rhd,rphd->rhp",
            queries.reshape(row_count, heads_here, HEAD),
            key_part,
            preferred_element_type=jnp.float32,
        )
        * scaling
    )
    highest = jnp.max(scores, axis=2)
    raw_weights = jnp.exp(scores - highest[:, :, None])
    totals = jnp.sum(raw_weights, axis=2)
    summed = jnp.einsum("rhp,rphd->rhd", raw_weights, value_part)
    return (highest, totals, summed)


def cross_attend(queries, cross_keys, cross_values, doc_length, scaling):
    query_rows = queries.shape[0]
    heads_here = cross_keys.shape[1]
    scores = (
        jnp.einsum(
            "qhd,jhd->hqj",
            queries.reshape(query_rows, heads_here, HEAD),
            cross_keys,
            preferred_element_type=jnp.float32,
        )
        * scaling
    )
    live_mask = lax.broadcasted_iota(jnp.int32, (1, 1, cross_keys.shape[0]), 2) < doc_length
    scores = jnp.where(live_mask, scores, -jnp.inf)
    highest = jnp.max(scores, axis=2, keepdims=True)
    raw_weights = jnp.exp(scores - highest)
    totals = jnp.sum(raw_weights, axis=2, keepdims=True)
    weights = (raw_weights / totals).astype(jnp.bfloat16)
    output = jnp.einsum("hqj,jhd->qhd", weights, cross_values, preferred_element_type=jnp.float32)
    return output.reshape(query_rows, heads_here * HEAD).astype(jnp.bfloat16)


def shards(
    step_embeds,
    lang_table,
    lang_ids,
    self_gain,
    self_wq,
    self_wk,
    self_wv,
    self_wo,
    cross_gain,
    cross_wq,
    cross_wkv,
    encoder_rows,
    doc_lengths,
    past_keys,
    past_values,
    parents,
):
    hyp_count = lax.axis_size("hyp")
    group_size = hyp_count // BEAMS
    my_index = lax.axis_index("hyp")
    my_beam = my_index // group_size
    my_slot = my_index % group_size
    row_count = step_embeds.shape[1]
    head_width = self_wq.shape[1]
    heads_here = head_width // HEAD
    doc_count = lang_ids.shape[0]
    scaling = HEAD ** (-0.5)
    my_langs = lax.dynamic_slice_in_dim(lang_ids, my_slot * BEAMS, BEAMS, 0).reshape(row_count)
    one_hot = (
        my_langs[:, None] == lax.broadcasted_iota(jnp.int32, (1, lang_table.shape[0]), 1)
    ).astype(jnp.bfloat16)
    lang_rows = jnp.dot(one_hot, lang_table, preferred_element_type=jnp.float32)
    full_weights = lax.all_gather(cross_wkv, "hyp", axis=0, tiled=True)
    cross_kv = jnp.dot(
        lax.all_gather(encoder_rows, "head", axis=1, tiled=True),
        full_weights,
        preferred_element_type=jnp.float32,
    ).astype(jnp.bfloat16)
    cross_kv = cross_kv.reshape(encoder_rows.shape[0], heads_here, 2, HEAD)
    cross_keys = cross_kv[:, :, 0, :]
    cross_values = cross_kv[:, :, 1, :]
    doc_length = doc_lengths[0]
    parent_view = parents.reshape(parents.shape[0], BEAMS, -1)
    my_parents = lax.dynamic_slice_in_dim(parent_view, my_slot * row_count, row_count, 2)
    own_parents = lax.dynamic_index_in_dim(my_parents, my_beam, 1, keepdims=False)
    contexts = []
    cache_stack = jnp.stack([past_keys, past_values])
    for step_idx in range(STEPS):
        offsets = (my_beam - own_parents[step_idx]) % BEAMS
        moved_list = [cache_stack]
        for peer_hop in range(1, BEAMS):
            moved_list.append(shifted(cache_stack, "hyp", peer_hop * group_size))
        cache_stack = pick_rows(moved_list, offsets, 1)
        start_hidden_in = step_embeds[step_idx].astype(jnp.float32) + lang_rows
        normed = rms_scaled(start_hidden_in, self_gain).astype(jnp.bfloat16)
        new_query = jnp.dot(normed, self_wq, preferred_element_type=jnp.float32).astype(
            jnp.bfloat16
        )
        new_key = jnp.dot(normed, self_wk, preferred_element_type=jnp.float32).astype(jnp.bfloat16)
        new_value = jnp.dot(normed, self_wv, preferred_element_type=jnp.float32).astype(
            jnp.bfloat16
        )
        fresh_rows = jnp.stack([new_key, new_value])[:, :, None, :]
        hidden_in, new_query, fresh_rows = (start_hidden_in, new_query, fresh_rows)
        cache_stack = jnp.concatenate([cache_stack, fresh_rows], axis=2)
        attn_parts = partial_attend(new_query, cache_stack, scaling)
        rows_here = hidden_in.shape[0]
        self_context = (
            (attn_parts[2] / attn_parts[1][:, :, None])
            .reshape(rows_here, head_width)
            .astype(jnp.bfloat16)
        )
        partial_out = jnp.dot(self_context, self_wo, preferred_element_type=jnp.float32)
        residual = hidden_in + lax.psum(partial_out.astype(jnp.bfloat16), "head").astype(
            jnp.float32
        )
        normed_cross = rms_scaled(residual, cross_gain).astype(jnp.bfloat16)
        cross_query = jnp.dot(normed_cross, cross_wq, preferred_element_type=jnp.float32).astype(
            jnp.bfloat16
        )
        every_query = lax.all_gather(cross_query, "hyp", axis=0, tiled=True)
        arranged = every_query.reshape(BEAMS, doc_count, TARGETS, head_width)
        doc_queries = lax.dynamic_index_in_dim(arranged, my_index, 1, keepdims=False)
        answer = cross_attend(
            doc_queries.reshape(BEAMS * TARGETS, head_width),
            cross_keys,
            cross_values,
            doc_length,
            scaling,
        )
        every_answer = lax.all_gather(answer, "hyp", axis=0, tiled=True)
        by_owner = every_answer.reshape(doc_count, BEAMS, TARGETS, head_width)
        my_block = lax.dynamic_slice_in_dim(by_owner, my_slot * BEAMS, BEAMS, 0)
        contexts.append(
            lax.dynamic_index_in_dim(my_block, my_beam, 1, keepdims=False).reshape(
                row_count, head_width
            )
        )
    return (jnp.stack(contexts), cache_stack[0], cache_stack[1])


def solution(mesh):
    return jax.shard_map(
        shards,
        mesh=mesh,
        in_specs=(
            P(None, "hyp", None),
            P(),
            P(),
            P(),
            P(None, "head"),
            P(None, "head"),
            P(None, "head"),
            P("head", None),
            P(),
            P(None, "head"),
            P("hyp", "head"),
            P("hyp", "head"),
            P("hyp"),
            P("hyp", None, "head"),
            P("hyp", None, "head"),
            P(),
        ),
        out_specs=(P(None, "hyp", "head"), P("hyp", None, "head"), P("hyp", None, "head")),
        check_vma=False,
    )
```

profile of v0, /device:TPU:1, one launch (start us, length us, event | category | flops | bytes accessed | tf_op | source)
XLA Modules:
  0.0 360.1 jit_solution(13073119696567710992)
XLA Ops:
  8.1 1.5 copy_bitcast_fusion
  10.4 3.6 collective-permute-start
  15.9 2.7 fusion.11
  20.4 1.0 fusion.5
  21.4 1.0 fusion.4
  22.4 2.8 fusion.9
  25.2 1.0 fusion.3
  27.1 8.9 %collective-permute-done = bf16[2,16,32,256]{3,1,2,0:T(8,128)(2,1)} collective-permute-done((bf16[2,16,32,256]{3,1,2,0:T(8,128)(2,1)}, bf16[2,16,32,256]{3,1,2,0:T(8,128)(2,1)}, u32[]{:S(2)}, u32[]{:S(2)}) %collective-permute-start) | collective-permute-done | bytes 524320 | tf_op jit(solution)/shard_map/ppermute | solution.py:16
  36.0 4.9 %collective-permute-done.2 = bf16[2,16,32,256]{3,1,2,0:T(8,128)(2,1)} collective-permute-done((bf16[2,16,32,256]{3,1,2,0:T(8,128)(2,1)}, bf16[2,16,32,256]{3,1,2,0:T(8,128)(2,1)}, u32[]{:S(2)}, u32[]{:S(2)}) %collective-permute-start.2) | collective-permute-done | bytes 524320 | tf_op jit(solution)/shard_map/ppermute | solution.py:16
  40.9 1.5 select_select_fusion.2
  43.0 1.0 collective-permute-start.5
  44.8 1.1 convolution_convert_fusion.2
  45.9 10.0 %collective-permute-done.3 = bf16[2,16,33,256]{3,1,2,0:T(8,128)(2,1)S(1)} collective-permute-done((bf16[2,16,33,256]{3,1,2,0:T(8,128)(2,1)S(1)}, bf16[2,16,33,256]{3,1,2,0:T(8,128)(2,1)S(1)}, u32[]{:S(2)}, u32[]{:S(2)}) %collective-permute-start.3) | collective-permute-done | bytes 540704 | tf_op jit(solution)/shard_map/ppermute | solution.py:16
  55.9 1.1 collective-permute-done.4
  57.0 12.9 %collective-permute-done.5 = bf16[2,16,33,256]{3,1,2,0:T(8,128)(2,1)S(1)} collective-permute-done((bf16[2,16,33,256]{3,1,2,0:T(8,128)(2,1)S(1)}, bf16[2,16,33,256]{3,1,2,0:T(8,128)(2,1)S(1)}, u32[]{:S(2)}, u32[]{:S(2)}) %collective-permute-start.5) | collective-permute-done | bytes 540704 | tf_op jit(solution)/shard_map/ppermute | solution.py:16
  70.7 1.0 collective-permute-start.8
  72.5 1.1 convolution_convert_fusion.1
  73.6 10.3 %collective-permute-done.6 = bf16[2,16,34,256]{3,1,2,0:T(8,128)(2,1)S(1)} collective-permute-done((bf16[2,16,34,256]{3,1,2,0:T(8,128)(2,1)S(1)}, bf16[2,16,34,256]{3,1,2,0:T(8,128)(2,1)S(1)}, u32[]{:S(2)}, u32[]{:S(2)}) %collective-permute-start.6) | collective-permute-done | bytes 557088 | tf_op jit(solution)/shard_map/ppermute | solution.py:16
  84.6 13.7 %collective-permute-done.8 = bf16[2,16,34,256]{3,1,2,0:T(8,128)(2,1)S(1)} collective-permute-done((bf16[2,16,34,256]{3,1,2,0:T(8,128)(2,1)S(1)}, bf16[2,16,34,256]{3,1,2,0:T(8,128)(2,1)S(1)}, u32[]{:S(2)}, u32[]{:S(2)}) %collective-permute-start.8) | collective-permute-done | bytes 557088 | tf_op jit(solution)/shard_map/ppermute | solution.py:16
  99.5 1.1 convolution_convert_fusion
  103.0 72.8 %all-reduce.3.cloned.1.call-done = (bf16[16,4096]{1,0:T(8,128)(2,1)}, bf16[16,4096]{1,0:T(8,128)(2,1)}, bf16[16,4096]{1,0:T(8,128)(2,1)}) async-done(((bf16[16,4096]{1,0:T(8,128)(2,1)}, bf16[16,4096]{1,0:T(8,128)(2,1)}, bf16[16,4096]{1,0:T(8,128)(2,1)}), (bf16[16,4096]{1,0:T(8,128)(2,1)}, bf16[16,4096]{1,0:T(8,128)(2,1)}, bf16[16,4096]{1,0:T(8,128)(2,1)})) %all-reduce.3.cloned.1.call-update) | async-done | bytes 393232 | tf_op jit(solution)/shard_map/psum | solution.py:151
  175.8 1.8 multiply_reduce_fusion.4
  177.6 2.1 convolution_convert_fusion.4
  179.7 37.9 %all_gather.30 = bf16[512,256]{1,0:T(8,128)(2,1)S(1)} all-gather(bf16[16,256]{1,0:T(8,128)(2,1)S(1)} %convolution_convert_fusion.4), channel_id=1, replica_groups=mesh['hyp'=32,'head'=8] {'hyp'}, dimensions={0}, use_global_device_ids=true | all-gather | bytes 270336 | tf_op jit(solution)/shard_map/all_gather | solution.py:158
  218.9 2.0 convolution_convert_fusion.8
  220.9 24.2 %all_gather.28 = bf16[512,256]{1,0:T(8,128)(2,1)S(1)} all-gather(bf16[16,256]{1,0:T(8,128)(2,1)S(1)} %convolution_convert_fusion.8), channel_id=1, replica_groups=mesh['hyp'=32,'head'=8] {'hyp'}, dimensions={0}, use_global_device_ids=true | all-gather | bytes 270336 | tf_op jit(solution)/shard_map/all_gather | solution.py:158
  245.8 2.0 convolution_convert_fusion.12
  247.8 22.6 %all_gather.26 = bf16[512,256]{1,0:T(8,128)(2,1)S(1)} all-gather(bf16[16,256]{1,0:T(8,128)(2,1)S(1)} %convolution_convert_fusion.12), channel_id=1, replica_groups=mesh['hyp'=32,'head'=8] {'hyp'}, dimensions={0}, use_global_device_ids=true | all-gather | bytes 270336 | tf_op jit(solution)/shard_map/all_gather | solution.py:158
  270.7 7.5 %convolution_convert_fusion.3 = bf16[768,512]{0,1:T(8,128)(2,1)S(1)} fusion(bf16[768,4096]{1,0:T(8,128)(2,1)} %all-gather.6.cloned.1.call-done, bf16[4096,512]{1,0:T(8,128)(2,1)} %all-gather.8.cloned.1.call-done), kind=kOutput, calls=%fused_computation.3 | convolution fusion | flops 3221618688 | bytes 11272192 | tf_op jit(solution)/shard_map/dot_general | solution.py:111
  278.9 24.5 %all-gather.2 = bf16[512,1,256]{2,0,1:T(8,128)(2,1)S(1)} all-gather(bf16[16,1,256]{2,0,1:T(8,128)(2,1)S(1)} %fusion.14), channel_id=4, replica_groups=mesh['hyp'=32,'head'=8] {'hyp'}, dimensions={0}, use_global_device_ids=true | all-gather | bytes 270336 | tf_op jit(solution)/shard_map/all_gather | solution.py:168
  304.2 22.7 %all-gather.1 = bf16[512,1,256]{2,0,1:T(8,128)(2,1)S(1)} all-gather(bf16[16,1,256]{2,0,1:T(8,128)(2,1)S(1)} %fusion.13), channel_id=3, replica_groups=mesh['hyp'=32,'head'=8] {'hyp'}, dimensions={0}, use_global_device_ids=true | all-gather | bytes 270336 | tf_op jit(solution)/shard_map/all_gather | solution.py:168
  327.7 24.3 %all-gather = bf16[512,1,256]{2,0,1:T(8,128)(2,1)S(1)} all-gather(bf16[16,1,256]{2,0,1:T(8,128)(2,1)S(1)} %fusion.12), channel_id=2, replica_groups=mesh['hyp'=32,'head'=8] {'hyp'}, dimensions={0}, use_global_device_ids=true | all-gather | bytes 270336 | tf_op jit(solution)/shard_map/all_gather | solution.py:168
  (137 shorter events, 16.9 us)
Async XLA Ops:
  8.0 36.8 %copy-start = (bf16[256,4096]{1,0:T(8,128)(2,1)S(1)}, bf16[256,4096]{1,0:T(8,128)(2,1)}, u32[]{:S(2)}) copy-start(bf16[256,4096]{1,0:T(8,128)(2,1)} %param.23) | copy-start | bytes 6291460
  8.0 7.0 %copy-start.22 = (s32[32,4]{0,1:T(4,128)S(1)}, s32[32,4]{0,1:T(4,128)}, u32[]{:S(2)}) copy-start(s32[32,4]{0,1:T(4,128)} %param.18) | copy-start | bytes 1540
  8.0 7.2 %copy-start.4 = (bf16[3,16,4096]{2,1,0:T(8,128)(2,1)S(1)}, bf16[3,16,4096]{2,1,0:T(8,128)(2,1)}, u32[]{:S(2)}) copy-start(bf16[3,16,4096]{2,1,0:T(8,128)(2,1)} %param.16) | copy-start | bytes 1179652
  8.0 7.2 %copy-start.24 = (bf16[8,4096]{1,0:T(8,128)(2,1)S(1)}, bf16[8,4096]{1,0:T(8,128)(2,1)}, u32[]{:S(2)}) copy-start(bf16[8,4096]{1,0:T(8,128)(2,1)} %param.17) | copy-start | bytes 196612
  8.0 7.7 %copy-start.17 = (f32[4096]{0:T(1024)S(1)}, f32[4096]{0:T(1024)}, u32[]{:S(2)}) copy-start(f32[4096]{0:T(1024)} %param.19) | copy-start | bytes 49156
  8.1 167.7 %all-reduce.3.cloned.1.call-start = ((), (), s32[]{:S(2)}) async-start(), calls=%async_computation.2 | async-start | bytes 786432 | tf_op jit(solution)/shard_map/psum | solution.py:151
  10.4 25.6 %collective-permute-start = (bf16[2,16,32,256]{3,1,2,0:T(8,128)(2,1)}, bf16[2,16,32,256]{3,1,2,0:T(8,128)(2,1)}, u32[]{:S(2)}, u32[]{:S(2)}) collective-permute-start(bf16[2,16,32,256]{3,1,2,0:T(8,128)(2,1)} %pad_maximum_fusion.2), channel_id=1, source_target_pairs={{64,0},{72,8},{80,16},{88,24},{96,32},{104,40},{112,48},{120,56},{... | collective-permute-start | bytes 1572872 | tf_op jit(solution)/shard_map/ppermute | solution.py:16
  14.0 22.0 %collective-permute-start.1 = (bf16[2,16,32,256]{3,1,2,0:T(8,128)(2,1)}, bf16[2,16,32,256]{3,1,2,0:T(8,128)(2,1)}, u32[]{:S(2)}, u32[]{:S(2)}) collective-permute-start(bf16[2,16,32,256]{3,1,2,0:T(8,128)(2,1)} %pad_maximum_fusion.2), channel_id=1, source_target_pairs={{128,0},{136,8},{144,16},{152,24},{160,32},{168,40},{176,48},{184,... | collective-permute-start | bytes 1572872 | tf_op jit(solution)/shard_map/ppermute | solution.py:16
  14.3 26.6 %collective-permute-start.2 = (bf16[2,16,32,256]{3,1,2,0:T(8,128)(2,1)}, bf16[2,16,32,256]{3,1,2,0:T(8,128)(2,1)}, u32[]{:S(2)}, u32[]{:S(2)}) collective-permute-start(bf16[2,16,32,256]{3,1,2,0:T(8,128)(2,1)} %pad_maximum_fusion.2), channel_id=1, source_target_pairs={{192,0},{200,8},{208,16},{216,24},{224,32},{232,40},{240,48},{248,... | collective-permute-start | bytes 1572872 | tf_op jit(solution)/shard_map/ppermute | solution.py:16
  15.3 3.4 copy-start.2
  15.9 3.7 %copy-start.5 = (bf16[16,4096]{1,0:T(8,128)(2,1)}, bf16[16,4096]{1,0:T(8,128)(2,1)S(1)}, u32[]{:S(2)}) copy-start(bf16[16,4096]{1,0:T(8,128)(2,1)S(1)} %get-tuple-element.24) | copy-start | bytes 393220
  15.9 3.7 %copy-start.1 = (bf16[4096,256]{1,0:T(8,128)(2,1)S(1)}, bf16[4096,256]{1,0:T(8,128)(2,1)}, u32[]{:S(2)}) copy-start(bf16[4096,256]{1,0:T(8,128)(2,1)} %param.22) | copy-start | bytes 6291460
  22.4 2.8 copy-start.3
  26.2 0.9 copy-start.14
  40.9 3.2 copy-start.20
  42.5 13.4 %collective-permute-start.3 = (bf16[2,16,33,256]{3,1,2,0:T(8,128)(2,1)S(1)}, bf16[2,16,33,256]{3,1,2,0:T(8,128)(2,1)S(1)}, u32[]{:S(2)}, u32[]{:S(2)}) collective-permute-start(bf16[2,16,33,256]{3,1,2,0:T(8,128)(2,1)S(1)} %pad_maximum_fusion.1), channel_id=1, source_target_pairs={{64,0},{72,8},{80,16},{88,24},{96,32},{104,40},{112,48},{120,56},{... | collective-permute-start | bytes 1622024 | tf_op jit(solution)/shard_map/ppermute | solution.py:16
  42.6 14.5 %collective-permute-start.4 = (bf16[2,16,33,256]{3,1,2,0:T(8,128)(2,1)S(1)}, bf16[2,16,33,256]{3,1,2,0:T(8,128)(2,1)S(1)}, u32[]{:S(2)}, u32[]{:S(2)}) collective-permute-start(bf16[2,16,33,256]{3,1,2,0:T(8,128)(2,1)S(1)} %pad_maximum_fusion.1), channel_id=1, source_target_pairs={{128,0},{136,8},{144,16},{152,24},{160,32},{168,40},{176,48},{184,... | collective-permute-start | bytes 1622024 | tf_op jit(solution)/shard_map/ppermute | solution.py:16
  43.0 26.9 %collective-permute-start.5 = (bf16[2,16,33,256]{3,1,2,0:T(8,128)(2,1)S(1)}, bf16[2,16,33,256]{3,1,2,0:T(8,128)(2,1)S(1)}, u32[]{:S(2)}, u32[]{:S(2)}) collective-permute-start(bf16[2,16,33,256]{3,1,2,0:T(8,128)(2,1)S(1)} %pad_maximum_fusion.1), channel_id=1, source_target_pairs={{192,0},{200,8},{208,16},{216,24},{224,32},{232,40},{240,48},{248,... | collective-permute-start | bytes 1622024 | tf_op jit(solution)/shard_map/ppermute | solution.py:16
  70.2 13.8 %collective-permute-start.6 = (bf16[2,16,34,256]{3,1,2,0:T(8,128)(2,1)S(1)}, bf16[2,16,34,256]{3,1,2,0:T(8,128)(2,1)S(1)}, u32[]{:S(2)}, u32[]{:S(2)}) collective-permute-start(bf16[2,16,34,256]{3,1,2,0:T(8,128)(2,1)S(1)} %pad_maximum_fusion), channel_id=1, source_target_pairs={{64,0},{72,8},{80,16},{88,24},{96,32},{104,40},{112,48},{120,56},{... | collective-permute-start | bytes 1671176 | tf_op jit(solution)/shard_map/ppermute | solution.py:16
  70.2 14.4 %collective-permute-start.7 = (bf16[2,16,34,256]{3,1,2,0:T(8,128)(2,1)S(1)}, bf16[2,16,34,256]{3,1,2,0:T(8,128)(2,1)S(1)}, u32[]{:S(2)}, u32[]{:S(2)}) collective-permute-start(bf16[2,16,34,256]{3,1,2,0:T(8,128)(2,1)S(1)} %pad_maximum_fusion), channel_id=1, source_target_pairs={{128,0},{136,8},{144,16},{152,24},{160,32},{168,40},{176,48},{184,... | collective-permute-start | bytes 1671176 | tf_op jit(solution)/shard_map/ppermute | solution.py:16
  70.7 27.6 %collective-permute-start.8 = (bf16[2,16,34,256]{3,1,2,0:T(8,128)(2,1)S(1)}, bf16[2,16,34,256]{3,1,2,0:T(8,128)(2,1)S(1)}, u32[]{:S(2)}, u32[]{:S(2)}) collective-permute-start(bf16[2,16,34,256]{3,1,2,0:T(8,128)(2,1)S(1)} %pad_maximum_fusion), channel_id=1, source_target_pairs={{192,0},{200,8},{208,16},{216,24},{224,32},{232,40},{240,48},{248,... | collective-permute-start | bytes 1671176 | tf_op jit(solution)/shard_map/ppermute | solution.py:16
  73.6 25.0 %copy-start.19 = (bf16[16,256,1]{1,0,2:T(8,128)(2,1)S(1)}, bf16[16,256,1]{1,0,2:T(8,128)(2,1)}, u32[]{:S(2)}) copy-start(bf16[16,256,1]{1,0,2:T(8,128)(2,1)} %fusion.9) | copy-start | bytes 24580
  98.6 0.9 copy-start.9
  99.5 78.1 %copy-start.10 = (f32[4096]{0:T(1024)S(1)}, f32[4096]{0:T(1024)}, u32[]{:S(2)}) copy-start(f32[4096]{0:T(1024)} %param.24) | copy-start | bytes 49156
  100.6 170.0 %all-gather.8.cloned.1.call-start = ((), (), s32[]{:S(2)}) async-start(), calls=%async_computation.1 | async-start | bytes 4325376 | tf_op jit(solution)/shard_map/all_gather | solution.py:110
  101.2 169.5 %all-gather.6.cloned.1.call-start = ((), (), s32[]{:S(2)}) async-start(), calls=%async_computation | async-start | bytes 7077888 | tf_op jit(solution)/shard_map/all_gather | solution.py:112
  175.8 43.1 %copy-start.8 = (bf16[16,4096]{1,0:T(8,128)(2,1)S(1)}, bf16[16,4096]{1,0:T(8,128)(2,1)}, u32[]{:S(2)}) copy-start(bf16[16,4096]{1,0:T(8,128)(2,1)} %get-tuple-element.11) | copy-start | bytes 393220
  179.7 66.1 %copy-start.7 = (bf16[16,4096]{1,0:T(8,128)(2,1)S(1)}, bf16[16,4096]{1,0:T(8,128)(2,1)}, u32[]{:S(2)}) copy-start(bf16[16,4096]{1,0:T(8,128)(2,1)} %get-tuple-element.10) | copy-start | bytes 393220
  217.7 28.1 %copy-start.23 = (f32[16]{0:T(128)S(1)}, f32[16]{0:T(128)}, u32[]{:S(2)}) copy-start(f32[16]{0:T(128)} %get-tuple-element.3) | copy-start | bytes 196
  270.6 7.6 %copy-start.12 = (bf16[16,256]{1,0:T(8,128)(2,1)S(1)}, bf16[16,256]{1,0:T(8,128)(2,1)}, u32[]{:S(2)}) copy-start(bf16[16,256]{1,0:T(8,128)(2,1)} %reshape.403) | copy-start | bytes 24580
  270.6 7.6 %copy-start.18 = (pred[768]{0:T(1024)(128)(4,1)S(1)}, pred[768]{0:T(1024)(128)(4,1)}, u32[]{:S(2)}) copy-start(pred[768]{0:T(1024)(128)(4,1)} %iota_compare_fusion.2) | copy-start | bytes 2308
  270.6 32.9 %copy-start.11 = (bf16[16,256]{1,0:T(8,128)(2,1)S(1)}, bf16[16,256]{1,0:T(8,128)(2,1)}, u32[]{:S(2)}) copy-start(bf16[16,256]{1,0:T(8,128)(2,1)} %reshape.398) | copy-start | bytes 24580
  (5 other events, 3.9 us)
Sparse Core Ops, SparseCore 0:
  100.7 74.9 all-reduce.2
Sparse Core Ops, SparseCore 1:
  103.7 52.1 all-gather.7
  157.5 73.3 all-gather.5
where the time goes:
time: 360 us
  blocking collectives  156 us (43%)
  waiting for transfers between devices  136 us (38%)
  matrix products  30.7 us (9%)
  between operations  16.7 us (5%)
  other arithmetic  8.37 us (2%)
  starting transfers between devices  7.79 us (2%)
  local copies, waits for them, and re-layouts  4.05 us (1%)
    all_gather x3, blocking collectives, shards(): every_query = lax.all_gather(cross_query, 'hyp', axis=0, tiled=True)  84.7 us
    psum x1, waiting for transfers between devices, shards(): lax.psum(partial_out.astype(jnp.bfloat16), 'head').astype(jnp.float32)  72.8 us
    all_gather x3, blocking collectives, shards(): every_answer = lax.all_gather(answer, 'hyp', axis=0, tiled=True)  71.4 us
    ppermute x9, waiting for transfers between devices, shifted(): return lax.ppermute(block, axis, route)  62.5 us
    ppermute x9, starting transfers between devices, shifted(): return lax.ppermute(block, axis, route)  7.67 us
    dot_general x1, matrix products, shards(): jnp.dot(lax.all_gather(encoder_rows, 'head', axis=1, tiled=True), full_we...  7.47 us
  transfers between devices with their start and end apart: 12, of which 9 were waited for; matrix products, arithmetic and copies ran while one was open for 7% of the time, Pallas kernels for 0%

commit v1 on v0

--- a/solution.py
+++ b/solution.py
@@ -165,7 +165,12 @@
             doc_length,
             scaling,
         )
-        every_answer = lax.all_gather(answer, "hyp", axis=0, tiled=True)
+        every_answer = jnp.concatenate(
+            jax.lax.all_to_all(
+                jnp.stack([answer for _ in range(jax.lax.psum(1, "hyp"))], axis=0), "hyp", 0, 0
+            ),
+            axis=0,
+        )
         by_owner = every_answer.reshape(doc_count, BEAMS, TARGETS, head_width)
         my_block = lax.dynamic_slice_in_dim(by_owner, my_slot * BEAMS, BEAMS, 0)
         contexts.append(

time: 360 us -> 329 us (0.914)
  blocking collectives: 156 us -> 84.7 us
  waiting for transfers between devices: 136 us -> 161 us
  starting transfers between devices: 7.79 us -> 20.3 us
    all_gather x3 -> x0, blocking collectives: 71.4 us -> none  [shards(): every_answer = lax.all_gather(answer, 'hyp', axis=0, tiled=True)]
    all_to_all x0 -> x3, waiting for transfers between devices: none -> 24.9 us  [shards(): jax.lax.all_to_all(jnp.stack([answer for _ in range(jax.lax.psum(1, 'hyp'...]
    all_to_all x0 -> x3, starting transfers between devices: none -> 12.5 us  [shards(): jax.lax.all_to_all(jnp.stack([answer for _ in range(jax.lax.psum(1, 'hyp'...]
  transfers between devices with their start and end apart: 12 -> 15, of which waited for: 9 -> 12; matrix products, arithmetic and copies ran while one was open for 7% -> 8% of each run, Pallas kernels for 0% -> 0%
where the time goes in v1:
time: 329 us
  waiting for transfers between devices  161 us (49%)
  blocking collectives  84.7 us (26%)
  matrix products  30.8 us (9%)
  starting transfers between devices  20.3 us (6%)
  between operations  16.7 us (5%)
  other arithmetic  8.45 us (3%)
  local copies, waits for them, and re-layouts  6.38 us (2%)
    all_gather x3, blocking collectives, shards(): every_query = lax.all_gather(cross_query, 'hyp', axis=0, tiled=True)  84.7 us
    psum x1, waiting for transfers between devices, shards(): lax.psum(partial_out.astype(jnp.bfloat16), 'head').astype(jnp.float32)  72.7 us
    ppermute x9, waiting for transfers between devices, shifted(): return lax.ppermute(block, axis, route)  62.5 us
    all_to_all x3, waiting for transfers between devices, shards(): jax.lax.all_to_all(jnp.stack([answer for _ in range(jax.lax.psum(1, 'hyp'...  24.9 us
    all_to_all x3, starting transfers between devices, shards(): jax.lax.all_to_all(jnp.stack([answer for _ in range(jax.lax.psum(1, 'hyp'...  12.5 us
    ppermute x9, starting transfers between devices, shifted(): return lax.ppermute(block, axis, route)  7.67 us
    dot_general x1, matrix products, shards(): jnp.dot(lax.all_gather(encoder_rows, 'head', axis=1, tiled=True), full_we...  7.47 us
  transfers between devices with their start and end apart: 15, of which 12 were waited for; matrix products, arithmetic and copies ran while one was open for 8% of the time, Pallas kernels for 0%

profile of v1, /device:TPU:1, one launch (start us, length us, event | category | flops | bytes accessed | tf_op | source)
XLA Modules:
  0.0 328.6 jit_solution(2811271808512658126)
XLA Ops:
  8.1 1.5 copy_bitcast_fusion
  10.4 3.6 %collective-permute-start = (bf16[2,16,32,256]{3,1,2,0:T(8,128)(2,1)}, bf16[2,16,32,256]{3,1,2,0:T(8,128)(2,1)}, u32[]{:S(2)}, u32[]{:S(2)}) collective-permute-start(bf16[2,16,32,256]{3,1,2,0:T(8,128)(2,1)} %pad_maximum_fusion.2), channel_id=1, source_target_pairs={{64,0},{72,8},{80,16},{88,24},{96,32},{104,40},{112,48},{120,56},{... | collective-permute-start | bytes 1572872 | tf_op jit(solution)/shard_map/ppermute | solution.py:16
  15.9 2.7 fusion.11
  22.4 2.8 fusion.9
  27.1 8.9 %collective-permute-done = bf16[2,16,32,256]{3,1,2,0:T(8,128)(2,1)} collective-permute-done((bf16[2,16,32,256]{3,1,2,0:T(8,128)(2,1)}, bf16[2,16,32,256]{3,1,2,0:T(8,128)(2,1)}, u32[]{:S(2)}, u32[]{:S(2)}) %collective-permute-start) | collective-permute-done | bytes 524320 | tf_op jit(solution)/shard_map/ppermute | solution.py:16
  36.0 4.9 %collective-permute-done.2 = bf16[2,16,32,256]{3,1,2,0:T(8,128)(2,1)} collective-permute-done((bf16[2,16,32,256]{3,1,2,0:T(8,128)(2,1)}, bf16[2,16,32,256]{3,1,2,0:T(8,128)(2,1)}, u32[]{:S(2)}, u32[]{:S(2)}) %collective-permute-start.2) | collective-permute-done | bytes 524320 | tf_op jit(solution)/shard_map/ppermute | solution.py:16
  40.9 1.5 select_select_fusion.2
  43.0 1.0 collective-permute-start.5
  44.8 1.1 convolution_convert_fusion.2
  45.9 10.0 %collective-permute-done.3 = bf16[2,16,33,256]{3,1,2,0:T(8,128)(2,1)S(1)} collective-permute-done((bf16[2,16,33,256]{3,1,2,0:T(8,128)(2,1)S(1)}, bf16[2,16,33,256]{3,1,2,0:T(8,128)(2,1)S(1)}, u32[]{:S(2)}, u32[]{:S(2)}) %collective-permute-start.3) | collective-permute-done | bytes 540704 | tf_op jit(solution)/shard_map/ppermute | solution.py:16
  55.9 1.1 collective-permute-done.4
  57.0 12.9 %collective-permute-done.5 = bf16[2,16,33,256]{3,1,2,0:T(8,128)(2,1)S(1)} collective-permute-done((bf16[2,16,33,256]{3,1,2,0:T(8,128)(2,1)S(1)}, bf16[2,16,33,256]{3,1,2,0:T(8,128)(2,1)S(1)}, u32[]{:S(2)}, u32[]{:S(2)}) %collective-permute-start.5) | collective-permute-done | bytes 540704 | tf_op jit(solution)/shard_map/ppermute | solution.py:16
  70.7 1.0 collective-permute-start.8
  72.5 1.1 convolution_convert_fusion.1
  73.6 10.3 %collective-permute-done.6 = bf16[2,16,34,256]{3,1,2,0:T(8,128)(2,1)S(1)} collective-permute-done((bf16[2,16,34,256]{3,1,2,0:T(8,128)(2,1)S(1)}, bf16[2,16,34,256]{3,1,2,0:T(8,128)(2,1)S(1)}, u32[]{:S(2)}, u32[]{:S(2)}) %collective-permute-start.6) | collective-permute-done | bytes 557088 | tf_op jit(solution)/shard_map/ppermute | solution.py:16
  84.6 13.7 %collective-permute-done.8 = bf16[2,16,34,256]{3,1,2,0:T(8,128)(2,1)S(1)} collective-permute-done((bf16[2,16,34,256]{3,1,2,0:T(8,128)(2,1)S(1)}, bf16[2,16,34,256]{3,1,2,0:T(8,128)(2,1)S(1)}, u32[]{:S(2)}, u32[]{:S(2)}) %collective-permute-start.8) | collective-permute-done | bytes 557088 | tf_op jit(solution)/shard_map/ppermute | solution.py:16
  99.5 1.1 convolution_convert_fusion
  103.0 72.7 %all-reduce.3.cloned.1.call-done = (bf16[16,4096]{1,0:T(8,128)(2,1)}, bf16[16,4096]{1,0:T(8,128)(2,1)}, bf16[16,4096]{1,0:T(8,128)(2,1)}) async-done(((bf16[16,4096]{1,0:T(8,128)(2,1)}, bf16[16,4096]{1,0:T(8,128)(2,1)}, bf16[16,4096]{1,0:T(8,128)(2,1)}), (bf16[16,4096]{1,0:T(8,128)(2,1)}, bf16[16,4096]{1,0:T(8,128)(2,1)}, bf16[16,4096]{1,0:T(8,128)(2,1)})) %all-reduce.3.cloned.1.call-update) | async-done | bytes 393232 | tf_op jit(solution)/shard_map/psum | solution.py:151
  175.8 1.9 multiply_reduce_fusion.4
  177.7 2.1 convolution_convert_fusion.4
  179.8 37.9 %all_gather.19 = bf16[512,256]{1,0:T(8,128)(2,1)S(1)} all-gather(bf16[16,256]{1,0:T(8,128)(2,1)S(1)} %convolution_convert_fusion.4), channel_id=1, replica_groups=mesh['hyp'=32,'head'=8] {'hyp'}, dimensions={0}, use_global_device_ids=true | all-gather | bytes 270336 | tf_op jit(solution)/shard_map/all_gather | solution.py:158
  219.0 2.0 convolution_convert_fusion.8
  221.0 24.2 %all_gather.18 = bf16[512,256]{1,0:T(8,128)(2,1)S(1)} all-gather(bf16[16,256]{1,0:T(8,128)(2,1)S(1)} %convolution_convert_fusion.8), channel_id=1, replica_groups=mesh['hyp'=32,'head'=8] {'hyp'}, dimensions={0}, use_global_device_ids=true | all-gather | bytes 270336 | tf_op jit(solution)/shard_map/all_gather | solution.py:158
  245.9 2.0 convolution_convert_fusion.12
  247.9 22.6 %all_gather.17 = bf16[512,256]{1,0:T(8,128)(2,1)S(1)} all-gather(bf16[16,256]{1,0:T(8,128)(2,1)S(1)} %convolution_convert_fusion.12), channel_id=1, replica_groups=mesh['hyp'=32,'head'=8] {'hyp'}, dimensions={0}, use_global_device_ids=true | all-gather | bytes 270336 | tf_op jit(solution)/shard_map/all_gather | solution.py:158
  270.7 7.5 %convolution_convert_fusion.3 = bf16[768,512]{0,1:T(8,128)(2,1)S(1)} fusion(bf16[768,4096]{1,0:T(8,128)(2,1)} %all-gather.3.cloned.1.call-done, bf16[4096,512]{1,0:T(8,128)(2,1)} %all-gather.5.cloned.1.call-done), kind=kOutput, calls=%fused_computation.3 | convolution fusion | flops 3221618688 | bytes 11272192 | tf_op jit(solution)/shard_map/dot_general | solution.py:111
  279.7 5.0 %all-to-all-start.2 = ((bf16[32,16,256]{2,1,0:T(8,128)(2,1)}), bf16[32,16,256]{2,1,0:T(8,128)(2,1)S(1)}, u32[]{:S(2)}, u32[]{:S(2)}) async-start(bf16[32,16,256]{2,1,0:T(8,128)(2,1)} %stack.46), calls=%async_computation.2 | async-start | bytes 524288 | tf_op jit(solution)/shard_map/all_to_all | solution.py:169
  285.8 7.8 %all-to-all-done.2 = bf16[32,16,256]{2,1,0:T(8,128)(2,1)S(1)} async-done(((bf16[32,16,256]{2,1,0:T(8,128)(2,1)}), bf16[32,16,256]{2,1,0:T(8,128)(2,1)S(1)}, u32[]{:S(2)}, u32[]{:S(2)}) %all-to-all-start.2) | async-done | bytes 262176 | tf_op jit(solution)/shard_map/all_to_all | solution.py:169
  294.3 3.8 %all-to-all-start.1 = ((bf16[32,16,256]{2,1,0:T(8,128)(2,1)}), bf16[32,16,256]{2,1,0:T(8,128)(2,1)S(1)}, u32[]{:S(2)}, u32[]{:S(2)}) async-start(bf16[32,16,256]{2,1,0:T(8,128)(2,1)} %stack.42), calls=%async_computation.1 | async-start | bytes 524288 | tf_op jit(solution)/shard_map/all_to_all | solution.py:169
  298.5 8.5 %all-to-all-done.1 = bf16[32,16,256]{2,1,0:T(8,128)(2,1)S(1)} async-done(((bf16[32,16,256]{2,1,0:T(8,128)(2,1)}), bf16[32,16,256]{2,1,0:T(8,128)(2,1)S(1)}, u32[]{:S(2)}, u32[]{:S(2)}) %all-to-all-start.1) | async-done | bytes 262176 | tf_op jit(solution)/shard_map/all_to_all | solution.py:169
  307.7 3.8 %all-to-all-start = ((bf16[32,16,256]{2,1,0:T(8,128)(2,1)}), bf16[32,16,256]{2,1,0:T(8,128)(2,1)S(1)}, u32[]{:S(2)}, u32[]{:S(2)}) async-start(bf16[32,16,256]{2,1,0:T(8,128)(2,1)} %stack.38), calls=%async_computation | async-start | bytes 524288 | tf_op jit(solution)/shard_map/all_to_all | solution.py:169
  311.8 8.6 %all-to-all-done = bf16[32,16,256]{2,1,0:T(8,128)(2,1)S(1)} async-done(((bf16[32,16,256]{2,1,0:T(8,128)(2,1)}), bf16[32,16,256]{2,1,0:T(8,128)(2,1)S(1)}, u32[]{:S(2)}, u32[]{:S(2)}) %all-to-all-start) | async-done | bytes 262176 | tf_op jit(solution)/shard_map/all_to_all | solution.py:169
  (146 shorter events, 22.3 us)
Async XLA Ops:
  8.0 36.8 %copy-start = (bf16[256,4096]{1,0:T(8,128)(2,1)S(1)}, bf16[256,4096]{1,0:T(8,128)(2,1)}, u32[]{:S(2)}) copy-start(bf16[256,4096]{1,0:T(8,128)(2,1)} %param.23) | copy-start | bytes 6291460
  8.0 7.0 %copy-start.22 = (s32[32,4]{0,1:T(4,128)S(1)}, s32[32,4]{0,1:T(4,128)}, u32[]{:S(2)}) copy-start(s32[32,4]{0,1:T(4,128)} %param.18) | copy-start | bytes 1540
  8.0 7.3 %copy-start.4 = (bf16[3,16,4096]{2,1,0:T(8,128)(2,1)S(1)}, bf16[3,16,4096]{2,1,0:T(8,128)(2,1)}, u32[]{:S(2)}) copy-start(bf16[3,16,4096]{2,1,0:T(8,128)(2,1)} %param.16) | copy-start | bytes 1179652
  8.0 7.2 %copy-start.24 = (bf16[8,4096]{1,0:T(8,128)(2,1)S(1)}, bf16[8,4096]{1,0:T(8,128)(2,1)}, u32[]{:S(2)}) copy-start(bf16[8,4096]{1,0:T(8,128)(2,1)} %param.17) | copy-start | bytes 196612
  8.0 7.7 %copy-start.17 = (f32[4096]{0:T(1024)S(1)}, f32[4096]{0:T(1024)}, u32[]{:S(2)}) copy-start(f32[4096]{0:T(1024)} %param.19) | copy-start | bytes 49156
  8.1 167.7 %all-reduce.3.cloned.1.call-start = ((), (), s32[]{:S(2)}) async-start(), calls=%async_computation.5 | async-start | bytes 786432 | tf_op jit(solution)/shard_map/psum | solution.py:151
  10.4 25.6 %collective-permute-start = (bf16[2,16,32,256]{3,1,2,0:T(8,128)(2,1)}, bf16[2,16,32,256]{3,1,2,0:T(8,128)(2,1)}, u32[]{:S(2)}, u32[]{:S(2)}) collective-permute-start(bf16[2,16,32,256]{3,1,2,0:T(8,128)(2,1)} %pad_maximum_fusion.2), channel_id=1, source_target_pairs={{64,0},{72,8},{80,16},{88,24},{96,32},{104,40},{112,48},{120,56},{... | collective-permute-start | bytes 1572872 | tf_op jit(solution)/shard_map/ppermute | solution.py:16
  14.0 22.0 %collective-permute-start.1 = (bf16[2,16,32,256]{3,1,2,0:T(8,128)(2,1)}, bf16[2,16,32,256]{3,1,2,0:T(8,128)(2,1)}, u32[]{:S(2)}, u32[]{:S(2)}) collective-permute-start(bf16[2,16,32,256]{3,1,2,0:T(8,128)(2,1)} %pad_maximum_fusion.2), channel_id=1, source_target_pairs={{128,0},{136,8},{144,16},{152,24},{160,32},{168,40},{176,48},{184,... | collective-permute-start | bytes 1572872 | tf_op jit(solution)/shard_map/ppermute | solution.py:16
  14.3 26.6 %collective-permute-start.2 = (bf16[2,16,32,256]{3,1,2,0:T(8,128)(2,1)}, bf16[2,16,32,256]{3,1,2,0:T(8,128)(2,1)}, u32[]{:S(2)}, u32[]{:S(2)}) collective-permute-start(bf16[2,16,32,256]{3,1,2,0:T(8,128)(2,1)} %pad_maximum_fusion.2), channel_id=1, source_target_pairs={{192,0},{200,8},{208,16},{216,24},{224,32},{232,40},{240,48},{248,... | collective-permute-start | bytes 1572872 | tf_op jit(solution)/shard_map/ppermute | solution.py:16
  15.3 3.4 %copy-start.2 = (bf16[4096,256]{1,0:T(8,128)(2,1)S(1)}, bf16[4096,256]{1,0:T(8,128)(2,1)}, u32[]{:S(2)}) copy-start(bf16[4096,256]{1,0:T(8,128)(2,1)} %param.21) | copy-start | bytes 6291460
  15.9 3.7 %copy-start.5 = (bf16[16,4096]{1,0:T(8,128)(2,1)}, bf16[16,4096]{1,0:T(8,128)(2,1)S(1)}, u32[]{:S(2)}) copy-start(bf16[16,4096]{1,0:T(8,128)(2,1)S(1)} %get-tuple-element.24) | copy-start | bytes 393220
  15.9 3.7 %copy-start.1 = (bf16[4096,256]{1,0:T(8,128)(2,1)S(1)}, bf16[4096,256]{1,0:T(8,128)(2,1)}, u32[]{:S(2)}) copy-start(bf16[4096,256]{1,0:T(8,128)(2,1)} %param.22) | copy-start | bytes 6291460
  40.9 3.2 copy-start.20
  42.5 13.4 %collective-permute-start.3 = (bf16[2,16,33,256]{3,1,2,0:T(8,128)(2,1)S(1)}, bf16[2,16,33,256]{3,1,2,0:T(8,128)(2,1)S(1)}, u32[]{:S(2)}, u32[]{:S(2)}) collective-permute-start(bf16[2,16,33,256]{3,1,2,0:T(8,128)(2,1)S(1)} %pad_maximum_fusion.1), channel_id=1, source_target_pairs={{64,0},{72,8},{80,16},{88,24},{96,32},{104,40},{112,48},{120,56},{... | collective-permute-start | bytes 1622024 | tf_op jit(solution)/shard_map/ppermute | solution.py:16
  42.6 14.5 %collective-permute-start.4 = (bf16[2,16,33,256]{3,1,2,0:T(8,128)(2,1)S(1)}, bf16[2,16,33,256]{3,1,2,0:T(8,128)(2,1)S(1)}, u32[]{:S(2)}, u32[]{:S(2)}) collective-permute-start(bf16[2,16,33,256]{3,1,2,0:T(8,128)(2,1)S(1)} %pad_maximum_fusion.1), channel_id=1, source_target_pairs={{128,0},{136,8},{144,16},{152,24},{160,32},{168,40},{176,48},{184,... | collective-permute-start | bytes 1622024 | tf_op jit(solution)/shard_map/ppermute | solution.py:16
  43.0 26.9 %collective-permute-start.5 = (bf16[2,16,33,256]{3,1,2,0:T(8,128)(2,1)S(1)}, bf16[2,16,33,256]{3,1,2,0:T(8,128)(2,1)S(1)}, u32[]{:S(2)}, u32[]{:S(2)}) collective-permute-start(bf16[2,16,33,256]{3,1,2,0:T(8,128)(2,1)S(1)} %pad_maximum_fusion.1), channel_id=1, source_target_pairs={{192,0},{200,8},{208,16},{216,24},{224,32},{232,40},{240,48},{248,... | collective-permute-start | bytes 1622024 | tf_op jit(solution)/shard_map/ppermute | solution.py:16
  70.2 13.8 %collective-permute-start.6 = (bf16[2,16,34,256]{3,1,2,0:T(8,128)(2,1)S(1)}, bf16[2,16,34,256]{3,1,2,0:T(8,128)(2,1)S(1)}, u32[]{:S(2)}, u32[]{:S(2)}) collective-permute-start(bf16[2,16,34,256]{3,1,2,0:T(8,128)(2,1)S(1)} %pad_maximum_fusion), channel_id=1, source_target_pairs={{64,0},{72,8},{80,16},{88,24},{96,32},{104,40},{112,48},{120,56},{... | collective-permute-start | bytes 1671176 | tf_op jit(solution)/shard_map/ppermute | solution.py:16
  70.3 14.4 %collective-permute-start.7 = (bf16[2,16,34,256]{3,1,2,0:T(8,128)(2,1)S(1)}, bf16[2,16,34,256]{3,1,2,0:T(8,128)(2,1)S(1)}, u32[]{:S(2)}, u32[]{:S(2)}) collective-permute-start(bf16[2,16,34,256]{3,1,2,0:T(8,128)(2,1)S(1)} %pad_maximum_fusion), channel_id=1, source_target_pairs={{128,0},{136,8},{144,16},{152,24},{160,32},{168,40},{176,48},{184,... | collective-permute-start | bytes 1671176 | tf_op jit(solution)/shard_map/ppermute | solution.py:16
  70.7 27.6 %collective-permute-start.8 = (bf16[2,16,34,256]{3,1,2,0:T(8,128)(2,1)S(1)}, bf16[2,16,34,256]{3,1,2,0:T(8,128)(2,1)S(1)}, u32[]{:S(2)}, u32[]{:S(2)}) collective-permute-start(bf16[2,16,34,256]{3,1,2,0:T(8,128)(2,1)S(1)} %pad_maximum_fusion), channel_id=1, source_target_pairs={{192,0},{200,8},{208,16},{216,24},{224,32},{232,40},{240,48},{248,... | collective-permute-start | bytes 1671176 | tf_op jit(solution)/shard_map/ppermute | solution.py:16
  73.6 25.0 %copy-start.19 = (bf16[16,256,1]{1,0,2:T(8,128)(2,1)S(1)}, bf16[16,256,1]{1,0,2:T(8,128)(2,1)}, u32[]{:S(2)}) copy-start(bf16[16,256,1]{1,0,2:T(8,128)(2,1)} %fusion.9) | copy-start | bytes 24580
  99.5 78.1 %copy-start.10 = (f32[4096]{0:T(1024)S(1)}, f32[4096]{0:T(1024)}, u32[]{:S(2)}) copy-start(f32[4096]{0:T(1024)} %param.24) | copy-start | bytes 49156
  100.6 170.1 %all-gather.5.cloned.1.call-start = ((), (), s32[]{:S(2)}) async-start(), calls=%async_computation.4 | async-start | bytes 4325376 | tf_op jit(solution)/shard_map/all_gather | solution.py:110
  101.2 169.5 %all-gather.3.cloned.1.call-start = ((), (), s32[]{:S(2)}) async-start(), calls=%async_computation.3 | async-start | bytes 7077888 | tf_op jit(solution)/shard_map/all_gather | solution.py:112
  175.8 43.2 %copy-start.8 = (bf16[16,4096]{1,0:T(8,128)(2,1)S(1)}, bf16[16,4096]{1,0:T(8,128)(2,1)}, u32[]{:S(2)}) copy-start(bf16[16,4096]{1,0:T(8,128)(2,1)} %get-tuple-element.11) | copy-start | bytes 393220
  179.8 66.1 %copy-start.7 = (bf16[16,4096]{1,0:T(8,128)(2,1)S(1)}, bf16[16,4096]{1,0:T(8,128)(2,1)}, u32[]{:S(2)}) copy-start(bf16[16,4096]{1,0:T(8,128)(2,1)} %get-tuple-element.10) | copy-start | bytes 393220
  217.7 28.1 %copy-start.23 = (f32[16]{0:T(128)S(1)}, f32[16]{0:T(128)}, u32[]{:S(2)}) copy-start(f32[16]{0:T(128)} %get-tuple-element.3) | copy-start | bytes 196
  270.6 7.6 %copy-start.12 = (bf16[16,256]{1,0:T(8,128)(2,1)S(1)}, bf16[16,256]{1,0:T(8,128)(2,1)}, u32[]{:S(2)}) copy-start(bf16[16,256]{1,0:T(8,128)(2,1)} %reshape.401) | copy-start | bytes 24580
  270.7 7.6 %copy-start.18 = (pred[768]{0:T(1024)(128)(4,1)S(1)}, pred[768]{0:T(1024)(128)(4,1)}, u32[]{:S(2)}) copy-start(pred[768]{0:T(1024)(128)(4,1)} %iota_compare_fusion.2) | copy-start | bytes 2308
  270.7 14.1 %copy-start.11 = (bf16[16,256]{1,0:T(8,128)(2,1)S(1)}, bf16[16,256]{1,0:T(8,128)(2,1)}, u32[]{:S(2)}) copy-start(bf16[16,256]{1,0:T(8,128)(2,1)} %reshape.397) | copy-start | bytes 24580
  279.7 13.9 %all-to-all-start.2 = ((bf16[32,16,256]{2,1,0:T(8,128)(2,1)}), bf16[32,16,256]{2,1,0:T(8,128)(2,1)S(1)}, u32[]{:S(2)}, u32[]{:S(2)}) async-start(bf16[32,16,256]{2,1,0:T(8,128)(2,1)} %stack.46), calls=%async_computation.2 | async-start | bytes 524288 | tf_op jit(solution)/shard_map/all_to_all | solution.py:169
  294.3 12.7 %all-to-all-start.1 = ((bf16[32,16,256]{2,1,0:T(8,128)(2,1)}), bf16[32,16,256]{2,1,0:T(8,128)(2,1)S(1)}, u32[]{:S(2)}, u32[]{:S(2)}) async-start(bf16[32,16,256]{2,1,0:T(8,128)(2,1)} %stack.42), calls=%async_computation.1 | async-start | bytes 524288 | tf_op jit(solution)/shard_map/all_to_all | solution.py:169
  307.7 12.7 %all-to-all-start = ((bf16[32,16,256]{2,1,0:T(8,128)(2,1)}), bf16[32,16,256]{2,1,0:T(8,128)(2,1)S(1)}, u32[]{:S(2)}, u32[]{:S(2)}) async-start(bf16[32,16,256]{2,1,0:T(8,128)(2,1)} %stack.38), calls=%async_computation | async-start | bytes 524288 | tf_op jit(solution)/shard_map/all_to_all | solution.py:169
  (8 other events, 8.5 us)
Sparse Core Ops, SparseCore 0:
  100.7 74.9 all-reduce.2
Sparse Core Ops, SparseCore 1:
  103.7 52.1 all-gather.4
  157.5 73.3 all-gather.2
